TPU v7x, 256 devices: a whole 4x4x8 slice. The times are simulated.
256 devices in a mesh: rad: 8 (over z_hi, core), azi: 32 (over y, x, z_lo).
Axes of the slice: x: 4, y: 4, z: 8 (z_hi: 4, z_lo: 2; z = z_hi * 2 + z_lo), core: 2. Of those that a mesh axis runs over, the one named last changes fastest.
Arguments:
- gas_state: float32 [4, 16, 512, 1024], P(None, None, 'azi', 'rad'), may hold values from -6 to 6
- sound_sq: float32 [16, 512, 1024], P(None, 'azi', 'rad'), may hold values from 0.5 to 2
- offsets: int32 [1024], P('rad'), may hold values from 0 to 511
Outputs:
- final_state: float32 [4, 16, 512, 1024], P(None, None, 'azi', 'rad')
All inputs are finite; a program needn't handle non-finite values.
Results may differ from a plain program's by a relative error of at most 0.00002.
Values sent between devices are 32-bit elements; how exact they have to be, the bound alone decides.
No kernel may reach another device: no remote copies, remote signals or barrier semaphores. Data moves between devices by JAX's collectives and lax.ppermute only.
A program may use at most 64 MiB of HBM per device.

v0:
```python
import jax
import jax.numpy as jnp
from jax import lax
from jax.sharding import PartitionSpec as P

ORDER = 4
STEPS = 2


TIME_STEP = 0.5
ANGULAR_RATE = 1.0
SHEAR_RATE = 1.5


def padded_2(cells, sides, width):
    for axis, dim in sides:
        count = lax.axis_size(axis)
        head = lax.slice_in_dim(cells, 0, width, axis=dim)
        tail = lax.slice_in_dim(cells, cells.shape[dim] - width, cells.shape[dim], axis=dim)
        cells = jnp.concatenate(
            [
                lax.ppermute(tail, axis, [(i, (i + 1) % count) for i in range(count)]),
                cells,
                lax.ppermute(head, axis, [((i + 1) % count, i) for i in range(count)]),
            ],
            axis=dim,
        )
    return cells


def shifted(shard, axis, by):
    peers = lax.axis_size(axis)
    return lax.ppermute(shard, axis, [(i, (i + by) % peers) for i in range(peers)])


def window(values, start, length, which_dim):
    return lax.slice_in_dim(values, start, start + length, axis=which_dim)


def diff_along(values, which_dim):
    length = values.shape[which_dim] - 4
    return (
        8.0 * (window(values, 3, length, which_dim) - window(values, 1, length, which_dim))
        - (window(values, 4, length, which_dim) - window(values, 0, length, which_dim))
    ) / 12.0


def diff_vertical(values):
    return (
        8.0 * (jnp.roll(values, -1, 0) - jnp.roll(values, 1, 0))
        - (jnp.roll(values, -2, 0) - jnp.roll(values, 2, 0))
    ) / 12.0


def inner_part(values):
    return values[:, 2:-2, 2:-2]


def operator_core(pressure, radial_flow, azimuth_flow, vertical_flow):
    density_rate = -(
        diff_along(radial_flow[:, 2:-2, :], 2)
        + diff_along(azimuth_flow[:, :, 2:-2], 1)
        + diff_vertical(inner_part(vertical_flow))
    )
    radial_rate = -diff_along(pressure[:, 2:-2, :], 2) + 2.0 * ANGULAR_RATE * inner_part(
        azimuth_flow
    )
    azimuth_rate = -diff_along(pressure[:, :, 2:-2], 1) - (
        2.0 - SHEAR_RATE
    ) * ANGULAR_RATE * inner_part(radial_flow)
    vertical_rate = -diff_vertical(inner_part(pressure))
    return jnp.stack([density_rate, radial_rate, azimuth_rate, vertical_rate])


def radial_keep(extent, margin_cells, row_count):
    global_row = (
        lax.axis_index("rad") * row_count - margin_cells + jnp.arange(extent, dtype=jnp.int32)
    )
    row_total = row_count * lax.axis_size("rad")
    return ((global_row >= 0) & (global_row < row_total)).astype(jnp.float32)


def taylor_shallow(state, sound_sq):
    row_count = state.shape[3]
    keep_mask = radial_keep(row_count + 4, 2, row_count)
    running = state
    series = state
    for degree in range(1, ORDER + 1):
        stacked = jnp.stack([sound_sq * series[0], series[1], series[2], series[3]])
        padded = padded_2(stacked, (("rad", 3), ("azi", 2)), 2) * keep_mask
        series = TIME_STEP / degree * operator_core(padded[0], padded[1], padded[2], padded[3])
        running = running + series
    return running


def barrel_roll(values, amounts, which_dim, bit_total):
    for bit_pos in range(bit_total):
        chosen = amounts >> bit_pos & 1 == 1
        values = jnp.where(chosen, jnp.roll(values, 1 << bit_pos, axis=which_dim), values)
    return values


def remap_doubling(state, offsets):
    azi_count = state.shape[2]
    tile_steps = offsets // azi_count
    cell_steps = offsets % azi_count
    left_block = shifted(state, "azi", 1)
    extended = jnp.concatenate([left_block, state], axis=2)
    extended = barrel_roll(
        extended, cell_steps[None, None, None, :], 2, (azi_count - 1).bit_length()
    )
    state = extended[:, :, azi_count:, :]
    bit_count = lax.axis_size("azi").bit_length() - 1
    for bit_pos in range(bit_count):
        distance = 1 << bit_pos
        moved_rows = shifted(state, "azi", distance)
        chosen = tile_steps >> bit_pos & 1 == 1
        state = jnp.where(chosen[None, None, None, :], moved_rows, state)
    return state


def per_device(gas_state, sound_sq, offsets):
    state = gas_state
    for timestep in range(STEPS):
        running = taylor_shallow(state, sound_sq)
        state = remap_doubling(running, offsets)
    return state


def solution(mesh):
    in_specs = (P(None, None, "azi", "rad"), P(None, "azi", "rad"), P("rad"))
    out_specs = P(None, None, "azi", "rad")
    return jax.shard_map(
        per_device, mesh=mesh, in_specs=in_specs, out_specs=out_specs, check_vma=False
    )
```

profile of v0, /device:TPU:64, one launch (start us, length us, event | category | flops | bytes accessed | tf_op | source)
XLA Modules:
  0.0 427.3 jit_solution(15090975386930208996)
XLA Ops:
  4.9 8.0 %collective-permute-done = f32[4,16,16,2]{3,2,1,0:T(8,128)S(1)} collective-permute-done((f32[4,16,16,2]{3,2,1,0:T(8,128)S(1)}, f32[4,16,16,2]{3,2,1,0:T(8,128)S(1)}, u32[]{:S(2)}, u32[]{:S(2)}) %collective-permute-start) | collective-permute-done | bytes 8224 | tf_op jit(solution)/shard_map/ppermute | solution.py:22
  19.5 4.7 %collective-permute-start.3 = (f32[4,16,2,132]{3,2,1,0:T(2,128)S(1)}, f32[4,16,2,132]{3,2,1,0:T(2,128)S(1)}, u32[]{:S(2)}, u32[]{:S(2)}) collective-permute-start(f32[4,16,2,132]{3,2,1,0:T(2,128)S(1)} %get-tuple-element.56), channel_id=1, source_target_pairs={{1,0},{2,1},{3,2},{4,3},{5,4},{6,5},{7,6},{8,7},{9,8},{10,9},{11,1... | collective-permute-start | bytes 202760 | tf_op jit(solution)/shard_map/ppermute | solution.py:24
  24.2 5.2 %collective-permute-done.2 = f32[4,16,2,132]{3,2,1,0:T(2,128)S(1)} collective-permute-done((f32[4,16,2,132]{3,2,1,0:T(2,128)S(1)}, f32[4,16,2,132]{3,2,1,0:T(2,128)S(1)}, u32[]{:S(2)}, u32[]{:S(2)}) %collective-permute-start.2) | collective-permute-done | bytes 67616 | tf_op jit(solution)/shard_map/ppermute | solution.py:22
  35.4 12.5 %collective-permute-done.4 = f32[4,16,16,2]{3,2,1,0:T(8,128)S(1)} collective-permute-done((f32[4,16,16,2]{3,2,1,0:T(8,128)S(1)}, f32[4,16,16,2]{3,2,1,0:T(8,128)S(1)}, u32[]{:S(2)}, u32[]{:S(2)}) %collective-permute-start.4) | collective-permute-done | bytes 8224 | tf_op jit(solution)/shard_map/ppermute | solution.py:22
  48.5 6.2 %collective-permute-start.7 = (f32[4,16,2,132]{3,2,1,0:T(2,128)S(1)}, f32[4,16,2,132]{3,2,1,0:T(2,128)S(1)}, u32[]{:S(2)}, u32[]{:S(2)}) collective-permute-start(f32[4,16,2,132]{3,2,1,0:T(2,128)S(1)} %get-tuple-element.50), channel_id=1, source_target_pairs={{1,0},{2,1},{3,2},{4,3},{5,4},{6,5},{7,6},{8,7},{9,8},{10,9},{11,1... | collective-permute-start | bytes 202760 | tf_op jit(solution)/shard_map/ppermute | solution.py:24
  60.9 7.3 %collective-permute-start.8 = (f32[4,16,16,2]{3,2,1,0:T(8,128)S(1)}, f32[4,16,16,2]{3,2,1,0:T(8,128)S(1)}, u32[]{:S(2)}, u32[]{:S(2)}) collective-permute-start(f32[4,16,16,2]{3,2,1,0:T(8,128)S(1)} %get-tuple-element.67), channel_id=1, source_target_pairs={{0,32},{32,64},{64,96},{96,128},{128,160},{160,192},{192,224},{224... | collective-permute-start | bytes 24584 | tf_op jit(solution)/shard_map/ppermute | solution.py:22
  68.2 8.2 %collective-permute-done.8 = f32[4,16,16,2]{3,2,1,0:T(8,128)S(1)} collective-permute-done((f32[4,16,16,2]{3,2,1,0:T(8,128)S(1)}, f32[4,16,16,2]{3,2,1,0:T(8,128)S(1)}, u32[]{:S(2)}, u32[]{:S(2)}) %collective-permute-start.8) | collective-permute-done | bytes 8224 | tf_op jit(solution)/shard_map/ppermute | solution.py:22
  77.0 8.6 %collective-permute-start.11 = (f32[4,16,2,132]{3,2,1,0:T(2,128)S(1)}, f32[4,16,2,132]{3,2,1,0:T(2,128)S(1)}, u32[]{:S(2)}, u32[]{:S(2)}) collective-permute-start(f32[4,16,2,132]{3,2,1,0:T(2,128)S(1)} %get-tuple-element.44), channel_id=1, source_target_pairs={{1,0},{2,1},{3,2},{4,3},{5,4},{6,5},{7,6},{8,7},{9,8},{10,9},{11,1... | collective-permute-start | bytes 202760 | tf_op jit(solution)/shard_map/ppermute | solution.py:24
  91.2 6.8 %collective-permute-start.12 = (f32[4,16,16,2]{3,2,1,0:T(8,128)S(1)}, f32[4,16,16,2]{3,2,1,0:T(8,128)S(1)}, u32[]{:S(2)}, u32[]{:S(2)}) collective-permute-start(f32[4,16,16,2]{3,2,1,0:T(8,128)S(1)} %get-tuple-element.65), channel_id=1, source_target_pairs={{0,32},{32,64},{64,96},{96,128},{128,160},{160,192},{192,224},{224... | collective-permute-start | bytes 24584 | tf_op jit(solution)/shard_map/ppermute | solution.py:22
  98.1 7.3 %collective-permute-done.12 = f32[4,16,16,2]{3,2,1,0:T(8,128)S(1)} collective-permute-done((f32[4,16,16,2]{3,2,1,0:T(8,128)S(1)}, f32[4,16,16,2]{3,2,1,0:T(8,128)S(1)}, u32[]{:S(2)}, u32[]{:S(2)}) %collective-permute-start.12) | collective-permute-done | bytes 8224 | tf_op jit(solution)/shard_map/ppermute | solution.py:22
  105.9 8.5 %collective-permute-start.15 = (f32[4,16,2,132]{3,2,1,0:T(2,128)S(1)}, f32[4,16,2,132]{3,2,1,0:T(2,128)S(1)}, u32[]{:S(2)}, u32[]{:S(2)}) collective-permute-start(f32[4,16,2,132]{3,2,1,0:T(2,128)S(1)} %get-tuple-element.38), channel_id=1, source_target_pairs={{1,0},{2,1},{3,2},{4,3},{5,4},{6,5},{7,6},{8,7},{9,8},{10,9},{11,1... | collective-permute-start | bytes 202760 | tf_op jit(solution)/shard_map/ppermute | solution.py:24
  121.4 18.8 %collective-permute-done.16 = f32[4,16,16,128]{3,2,1,0:T(8,128)S(1)} collective-permute-done((f32[4,16,16,128]{3,2,1,0:T(8,128)S(1)}, f32[4,16,16,128]{3,2,1,0:T(8,128)S(1)}, u32[]{:S(2)}, u32[]{:S(2)}) %collective-permute-start.16) | collective-permute-done | bytes 524320 | tf_op jit(solution)/shard_map/ppermute | solution.py:33
  141.6 18.2 %collective-permute-done.17 = f32[4,16,16,128]{3,2,1,0:T(8,128)S(1)} collective-permute-done((f32[4,16,16,128]{3,2,1,0:T(8,128)S(1)}, f32[4,16,16,128]{3,2,1,0:T(8,128)S(1)}, u32[]{:S(2)}, u32[]{:S(2)}) %collective-permute-start.17) | collective-permute-done | bytes 524320 | tf_op jit(solution)/shard_map/ppermute | solution.py:33
  160.0 16.5 %collective-permute-done.18 = f32[4,16,16,128]{3,2,1,0:T(8,128)S(1)} collective-permute-done((f32[4,16,16,128]{3,2,1,0:T(8,128)S(1)}, f32[4,16,16,128]{3,2,1,0:T(8,128)S(1)}, u32[]{:S(2)}, u32[]{:S(2)}) %collective-permute-start.18) | collective-permute-done | bytes 524320 | tf_op jit(solution)/shard_map/ppermute | solution.py:33
  176.6 15.9 %collective-permute-done.19 = f32[4,16,16,128]{3,2,1,0:T(8,128)S(1)} collective-permute-done((f32[4,16,16,128]{3,2,1,0:T(8,128)S(1)}, f32[4,16,16,128]{3,2,1,0:T(8,128)S(1)}, u32[]{:S(2)}, u32[]{:S(2)}) %collective-permute-start.19) | collective-permute-done | bytes 524320 | tf_op jit(solution)/shard_map/ppermute | solution.py:33
  192.7 12.6 %collective-permute-done.20 = f32[4,16,16,128]{3,2,1,0:T(8,128)S(1)} collective-permute-done((f32[4,16,16,128]{3,2,1,0:T(8,128)S(1)}, f32[4,16,16,128]{3,2,1,0:T(8,128)S(1)}, u32[]{:S(2)}, u32[]{:S(2)}) %collective-permute-start.20) | collective-permute-done | bytes 524320 | tf_op jit(solution)/shard_map/ppermute | solution.py:33
  205.5 12.1 %collective-permute-done.21 = f32[4,16,16,128]{3,2,1,0:T(8,128)S(1)} collective-permute-done((f32[4,16,16,128]{3,2,1,0:T(8,128)S(1)}, f32[4,16,16,128]{3,2,1,0:T(8,128)S(1)}, u32[]{:S(2)}, u32[]{:S(2)}) %collective-permute-start.21) | collective-permute-done | bytes 524320 | tf_op jit(solution)/shard_map/ppermute | solution.py:33
  220.6 10.4 %collective-permute-done.22 = f32[4,16,16,2]{3,2,1,0:T(8,128)S(1)} collective-permute-done((f32[4,16,16,2]{3,2,1,0:T(8,128)S(1)}, f32[4,16,16,2]{3,2,1,0:T(8,128)S(1)}, u32[]{:S(2)}, u32[]{:S(2)}) %collective-permute-start.22) | collective-permute-done | bytes 8224 | tf_op jit(solution)/shard_map/ppermute | solution.py:22
  231.6 6.2 %collective-permute-start.25 = (f32[4,16,2,132]{3,2,1,0:T(2,128)S(1)}, f32[4,16,2,132]{3,2,1,0:T(2,128)S(1)}, u32[]{:S(2)}, u32[]{:S(2)}) collective-permute-start(f32[4,16,2,132]{3,2,1,0:T(2,128)S(1)} %get-tuple-element.32), channel_id=1, source_target_pairs={{1,0},{2,1},{3,2},{4,3},{5,4},{6,5},{7,6},{8,7},{9,8},{10,9},{11,1... | collective-permute-start | bytes 202760 | tf_op jit(solution)/shard_map/ppermute | solution.py:24
  246.6 11.1 %collective-permute-done.26 = f32[4,16,16,2]{3,2,1,0:T(8,128)S(1)} collective-permute-done((f32[4,16,16,2]{3,2,1,0:T(8,128)S(1)}, f32[4,16,16,2]{3,2,1,0:T(8,128)S(1)}, u32[]{:S(2)}, u32[]{:S(2)}) %collective-permute-start.26) | collective-permute-done | bytes 8224 | tf_op jit(solution)/shard_map/ppermute | solution.py:22
  258.3 6.2 %collective-permute-start.29 = (f32[4,16,2,132]{3,2,1,0:T(2,128)S(1)}, f32[4,16,2,132]{3,2,1,0:T(2,128)S(1)}, u32[]{:S(2)}, u32[]{:S(2)}) collective-permute-start(f32[4,16,2,132]{3,2,1,0:T(2,128)S(1)} %get-tuple-element.26), channel_id=1, source_target_pairs={{1,0},{2,1},{3,2},{4,3},{5,4},{6,5},{7,6},{8,7},{9,8},{10,9},{11,1... | collective-permute-start | bytes 202760 | tf_op jit(solution)/shard_map/ppermute | solution.py:24
  274.4 12.5 %collective-permute-done.30 = f32[4,16,16,2]{3,2,1,0:T(8,128)S(1)} collective-permute-done((f32[4,16,16,2]{3,2,1,0:T(8,128)S(1)}, f32[4,16,16,2]{3,2,1,0:T(8,128)S(1)}, u32[]{:S(2)}, u32[]{:S(2)}) %collective-permute-start.30) | collective-permute-done | bytes 8224 | tf_op jit(solution)/shard_map/ppermute | solution.py:22
  287.4 6.2 %collective-permute-start.33 = (f32[4,16,2,132]{3,2,1,0:T(2,128)S(1)}, f32[4,16,2,132]{3,2,1,0:T(2,128)S(1)}, u32[]{:S(2)}, u32[]{:S(2)}) collective-permute-start(f32[4,16,2,132]{3,2,1,0:T(2,128)S(1)} %get-tuple-element.20), channel_id=1, source_target_pairs={{1,0},{2,1},{3,2},{4,3},{5,4},{6,5},{7,6},{8,7},{9,8},{10,9},{11,1... | collective-permute-start | bytes 202760 | tf_op jit(solution)/shard_map/ppermute | solution.py:24
  298.0 5.0 %collective-permute-done.33 = f32[4,16,2,132]{3,2,1,0:T(2,128)S(1)} collective-permute-done((f32[4,16,2,132]{3,2,1,0:T(2,128)S(1)}, f32[4,16,2,132]{3,2,1,0:T(2,128)S(1)}, u32[]{:S(2)}, u32[]{:S(2)}) %collective-permute-start.33) | collective-permute-done | bytes 67616 | tf_op jit(solution)/shard_map/ppermute | solution.py:24
  308.8 8.0 %collective-permute-done.34 = f32[4,16,16,2]{3,2,1,0:T(8,128)S(1)} collective-permute-done((f32[4,16,16,2]{3,2,1,0:T(8,128)S(1)}, f32[4,16,16,2]{3,2,1,0:T(8,128)S(1)}, u32[]{:S(2)}, u32[]{:S(2)}) %collective-permute-start.34) | collective-permute-done | bytes 8224 | tf_op jit(solution)/shard_map/ppermute | solution.py:22
  317.4 6.2 %collective-permute-start.37 = (f32[4,16,2,132]{3,2,1,0:T(2,128)S(1)}, f32[4,16,2,132]{3,2,1,0:T(2,128)S(1)}, u32[]{:S(2)}, u32[]{:S(2)}) collective-permute-start(f32[4,16,2,132]{3,2,1,0:T(2,128)S(1)} %get-tuple-element.14), channel_id=1, source_target_pairs={{1,0},{2,1},{3,2},{4,3},{5,4},{6,5},{7,6},{8,7},{9,8},{10,9},{11,1... | collective-permute-start | bytes 202760 | tf_op jit(solution)/shard_map/ppermute | solution.py:24
  330.1 18.9 %collective-permute-done.38 = f32[4,16,16,128]{3,2,1,0:T(8,128)S(1)} collective-permute-done((f32[4,16,16,128]{3,2,1,0:T(8,128)S(1)}, f32[4,16,16,128]{3,2,1,0:T(8,128)S(1)}, u32[]{:S(2)}, u32[]{:S(2)}) %collective-permute-start.38) | collective-permute-done | bytes 524320 | tf_op jit(solution)/shard_map/ppermute | solution.py:33
  350.3 18.1 %collective-permute-done.39 = f32[4,16,16,128]{3,2,1,0:T(8,128)S(1)} collective-permute-done((f32[4,16,16,128]{3,2,1,0:T(8,128)S(1)}, f32[4,16,16,128]{3,2,1,0:T(8,128)S(1)}, u32[]{:S(2)}, u32[]{:S(2)}) %collective-permute-start.39) | collective-permute-done | bytes 524320 | tf_op jit(solution)/shard_map/ppermute | solution.py:33
  368.7 16.4 %collective-permute-done.40 = f32[4,16,16,128]{3,2,1,0:T(8,128)S(1)} collective-permute-done((f32[4,16,16,128]{3,2,1,0:T(8,128)S(1)}, f32[4,16,16,128]{3,2,1,0:T(8,128)S(1)}, u32[]{:S(2)}, u32[]{:S(2)}) %collective-permute-start.40) | collective-permute-done | bytes 524320 | tf_op jit(solution)/shard_map/ppermute | solution.py:33
  385.2 15.8 %collective-permute-done.41 = f32[4,16,16,128]{3,2,1,0:T(8,128)S(1)} collective-permute-done((f32[4,16,16,128]{3,2,1,0:T(8,128)S(1)}, f32[4,16,16,128]{3,2,1,0:T(8,128)S(1)}, u32[]{:S(2)}, u32[]{:S(2)}) %collective-permute-start.41) | collective-permute-done | bytes 524320 | tf_op jit(solution)/shard_map/ppermute | solution.py:33
  401.2 12.6 %collective-permute-done.42 = f32[4,16,16,128]{3,2,1,0:T(8,128)S(1)} collective-permute-done((f32[4,16,16,128]{3,2,1,0:T(8,128)S(1)}, f32[4,16,16,128]{3,2,1,0:T(8,128)S(1)}, u32[]{:S(2)}, u32[]{:S(2)}) %collective-permute-start.42) | collective-permute-done | bytes 524320 | tf_op jit(solution)/shard_map/ppermute | solution.py:33
  414.0 12.0 %collective-permute-done.43 = f32[4,16,16,128]{3,2,1,0:T(8,128)S(1)} collective-permute-done((f32[4,16,16,128]{3,2,1,0:T(8,128)S(1)}, f32[4,16,16,128]{3,2,1,0:T(8,128)S(1)}, u32[]{:S(2)}, u32[]{:S(2)}) %collective-permute-start.43) | collective-permute-done | bytes 524320 | tf_op jit(solution)/shard_map/ppermute | solution.py:33
  (240 shorter events, 82.5 us)
Async XLA Ops:
  2.2 10.7 %collective-permute-start = (f32[4,16,16,2]{3,2,1,0:T(8,128)S(1)}, f32[4,16,16,2]{3,2,1,0:T(8,128)S(1)}, u32[]{:S(2)}, u32[]{:S(2)}) collective-permute-start(f32[4,16,16,2]{3,2,1,0:T(8,128)S(1)} %get-tuple-element.71), channel_id=1, source_target_pairs={{0,32},{32,64},{64,96},{96,128},{128,160},{160,192},{192,224},{224... | collective-permute-start | bytes 24584 | tf_op jit(solution)/shard_map/ppermute | solution.py:22
  2.3 15.0 %collective-permute-start.1 = (f32[4,16,16,2]{3,2,1,0:T(8,128)S(1)}, f32[4,16,16,2]{3,2,1,0:T(8,128)S(1)}, u32[]{:S(2)}, u32[]{:S(2)}) collective-permute-start(f32[4,16,16,2]{3,2,1,0:T(8,128)S(1)} %get-tuple-element.72), channel_id=1, source_target_pairs={{32,0},{64,32},{96,64},{128,96},{160,128},{192,160},{224,192},{0,2... | collective-permute-start | bytes 24584 | tf_op jit(solution)/shard_map/ppermute | solution.py:24
  17.8 11.6 %collective-permute-start.2 = (f32[4,16,2,132]{3,2,1,0:T(2,128)S(1)}, f32[4,16,2,132]{3,2,1,0:T(2,128)S(1)}, u32[]{:S(2)}, u32[]{:S(2)}) collective-permute-start(f32[4,16,2,132]{3,2,1,0:T(2,128)S(1)} %get-tuple-element.55), channel_id=1, source_target_pairs={{0,1},{1,2},{2,3},{3,4},{4,5},{5,6},{6,7},{7,8},{8,9},{9,10},{10,1... | collective-permute-start | bytes 202760 | tf_op jit(solution)/shard_map/ppermute | solution.py:22
  32.7 15.2 %collective-permute-start.4 = (f32[4,16,16,2]{3,2,1,0:T(8,128)S(1)}, f32[4,16,16,2]{3,2,1,0:T(8,128)S(1)}, u32[]{:S(2)}, u32[]{:S(2)}) collective-permute-start(f32[4,16,16,2]{3,2,1,0:T(8,128)S(1)} %get-tuple-element.69), channel_id=1, source_target_pairs={{0,32},{32,64},{64,96},{96,128},{128,160},{160,192},{192,224},{224... | collective-permute-start | bytes 24584 | tf_op jit(solution)/shard_map/ppermute | solution.py:22
  35.4 12.5 %collective-permute-start.5 = (f32[4,16,16,2]{3,2,1,0:T(8,128)S(1)}, f32[4,16,16,2]{3,2,1,0:T(8,128)S(1)}, u32[]{:S(2)}, u32[]{:S(2)}) collective-permute-start(f32[4,16,16,2]{3,2,1,0:T(8,128)S(1)} %get-tuple-element.70), channel_id=1, source_target_pairs={{32,0},{64,32},{96,64},{128,96},{160,128},{192,160},{224,192},{0,2... | collective-permute-start | bytes 24584 | tf_op jit(solution)/shard_map/ppermute | solution.py:24
  60.9 15.5 %collective-permute-start.8 = (f32[4,16,16,2]{3,2,1,0:T(8,128)S(1)}, f32[4,16,16,2]{3,2,1,0:T(8,128)S(1)}, u32[]{:S(2)}, u32[]{:S(2)}) collective-permute-start(f32[4,16,16,2]{3,2,1,0:T(8,128)S(1)} %get-tuple-element.67), channel_id=1, source_target_pairs={{0,32},{32,64},{64,96},{96,128},{128,160},{160,192},{192,224},{224... | collective-permute-start | bytes 24584 | tf_op jit(solution)/shard_map/ppermute | solution.py:22
  76.9 11.5 %collective-permute-start.10 = (f32[4,16,2,132]{3,2,1,0:T(2,128)S(1)}, f32[4,16,2,132]{3,2,1,0:T(2,128)S(1)}, u32[]{:S(2)}, u32[]{:S(2)}) collective-permute-start(f32[4,16,2,132]{3,2,1,0:T(2,128)S(1)} %get-tuple-element.43), channel_id=1, source_target_pairs={{0,1},{1,2},{2,3},{3,4},{4,5},{5,6},{6,7},{7,8},{8,9},{9,10},{10,1... | collective-permute-start | bytes 202760 | tf_op jit(solution)/shard_map/ppermute | solution.py:22
  77.0 11.4 %collective-permute-start.11 = (f32[4,16,2,132]{3,2,1,0:T(2,128)S(1)}, f32[4,16,2,132]{3,2,1,0:T(2,128)S(1)}, u32[]{:S(2)}, u32[]{:S(2)}) collective-permute-start(f32[4,16,2,132]{3,2,1,0:T(2,128)S(1)} %get-tuple-element.44), channel_id=1, source_target_pairs={{1,0},{2,1},{3,2},{4,3},{5,4},{6,5},{7,6},{8,7},{9,8},{10,9},{11,1... | collective-permute-start | bytes 202760 | tf_op jit(solution)/shard_map/ppermute | solution.py:24
  91.2 14.1 %collective-permute-start.12 = (f32[4,16,16,2]{3,2,1,0:T(8,128)S(1)}, f32[4,16,16,2]{3,2,1,0:T(8,128)S(1)}, u32[]{:S(2)}, u32[]{:S(2)}) collective-permute-start(f32[4,16,16,2]{3,2,1,0:T(8,128)S(1)} %get-tuple-element.65), channel_id=1, source_target_pairs={{0,32},{32,64},{64,96},{96,128},{128,160},{160,192},{192,224},{224... | collective-permute-start | bytes 24584 | tf_op jit(solution)/shard_map/ppermute | solution.py:22
  105.8 11.7 %collective-permute-start.14 = (f32[4,16,2,132]{3,2,1,0:T(2,128)S(1)}, f32[4,16,2,132]{3,2,1,0:T(2,128)S(1)}, u32[]{:S(2)}, u32[]{:S(2)}) collective-permute-start(f32[4,16,2,132]{3,2,1,0:T(2,128)S(1)} %get-tuple-element.37), channel_id=1, source_target_pairs={{0,1},{1,2},{2,3},{3,4},{4,5},{5,6},{6,7},{7,8},{8,9},{9,10},{10,1... | collective-permute-start | bytes 202760 | tf_op jit(solution)/shard_map/ppermute | solution.py:22
  105.9 11.6 %collective-permute-start.15 = (f32[4,16,2,132]{3,2,1,0:T(2,128)S(1)}, f32[4,16,2,132]{3,2,1,0:T(2,128)S(1)}, u32[]{:S(2)}, u32[]{:S(2)}) collective-permute-start(f32[4,16,2,132]{3,2,1,0:T(2,128)S(1)} %get-tuple-element.38), channel_id=1, source_target_pairs={{1,0},{2,1},{3,2},{4,3},{5,4},{6,5},{7,6},{8,7},{9,8},{10,9},{11,1... | collective-permute-start | bytes 202760 | tf_op jit(solution)/shard_map/ppermute | solution.py:24
  120.9 19.3 %collective-permute-start.16 = (f32[4,16,16,128]{3,2,1,0:T(8,128)S(1)}, f32[4,16,16,128]{3,2,1,0:T(8,128)S(1)}, u32[]{:S(2)}, u32[]{:S(2)}) collective-permute-start(f32[4,16,16,128]{3,2,1,0:T(8,128)S(1)} %fusion.4), channel_id=1, source_target_pairs={{0,1},{1,2},{2,3},{3,4},{4,5},{5,6},{6,7},{7,8},{8,9},{9,10},{10,1... | collective-permute-start | bytes 1572872 | tf_op jit(solution)/shard_map/ppermute | solution.py:33
  141.5 18.3 %collective-permute-start.17 = (f32[4,16,16,128]{3,2,1,0:T(8,128)S(1)}, f32[4,16,16,128]{3,2,1,0:T(8,128)S(1)}, u32[]{:S(2)}, u32[]{:S(2)}) collective-permute-start(f32[4,16,16,128]{3,2,1,0:T(8,128)S(1)} %slice_select_fusion.1), channel_id=1, source_target_pairs={{0,1},{1,2},{2,3},{3,4},{4,5},{5,6},{6,7},{7,8},{8,9},{9,10},{10,1... | collective-permute-start | bytes 1572872 | tf_op jit(solution)/shard_map/ppermute | solution.py:33
  159.9 16.6 %collective-permute-start.18 = (f32[4,16,16,128]{3,2,1,0:T(8,128)S(1)}, f32[4,16,16,128]{3,2,1,0:T(8,128)S(1)}, u32[]{:S(2)}, u32[]{:S(2)}) collective-permute-start(f32[4,16,16,128]{3,2,1,0:T(8,128)S(1)} %broadcast_select_fusion.1), channel_id=1, source_target_pairs={{0,2},{1,3},{2,4},{3,5},{4,6},{5,7},{6,8},{7,9},{8,10},{9,11},{10,... | collective-permute-start | bytes 1572872 | tf_op jit(solution)/shard_map/ppermute | solution.py:33
  176.5 16.0 %collective-permute-start.19 = (f32[4,16,16,128]{3,2,1,0:T(8,128)S(1)}, f32[4,16,16,128]{3,2,1,0:T(8,128)S(1)}, u32[]{:S(2)}, u32[]{:S(2)}) collective-permute-start(f32[4,16,16,128]{3,2,1,0:T(8,128)S(1)} %broadcast_select_fusion.3), channel_id=1, source_target_pairs={{0,4},{1,5},{2,6},{3,7},{4,8},{5,9},{6,10},{7,11},{8,12},{9,13},{1... | collective-permute-start | bytes 1572872 | tf_op jit(solution)/shard_map/ppermute | solution.py:33
  192.6 12.7 %collective-permute-start.20 = (f32[4,16,16,128]{3,2,1,0:T(8,128)S(1)}, f32[4,16,16,128]{3,2,1,0:T(8,128)S(1)}, u32[]{:S(2)}, u32[]{:S(2)}) collective-permute-start(f32[4,16,16,128]{3,2,1,0:T(8,128)S(1)} %broadcast_select_fusion.5), channel_id=1, source_target_pairs={{0,8},{1,9},{2,10},{3,11},{4,12},{5,13},{6,14},{7,15},{8,16},{9,17... | collective-permute-start | bytes 1572872 | tf_op jit(solution)/shard_map/ppermute | solution.py:33
  205.4 12.2 %collective-permute-start.21 = (f32[4,16,16,128]{3,2,1,0:T(8,128)S(1)}, f32[4,16,16,128]{3,2,1,0:T(8,128)S(1)}, u32[]{:S(2)}, u32[]{:S(2)}) collective-permute-start(f32[4,16,16,128]{3,2,1,0:T(8,128)S(1)} %broadcast_select_fusion.7), channel_id=1, source_target_pairs={{0,16},{1,17},{2,18},{3,19},{4,20},{5,21},{6,22},{7,23},{8,24},{9,... | collective-permute-start | bytes 1572872 | tf_op jit(solution)/shard_map/ppermute | solution.py:33
  217.9 13.2 %collective-permute-start.22 = (f32[4,16,16,2]{3,2,1,0:T(8,128)S(1)}, f32[4,16,16,2]{3,2,1,0:T(8,128)S(1)}, u32[]{:S(2)}, u32[]{:S(2)}) collective-permute-start(f32[4,16,16,2]{3,2,1,0:T(8,128)S(1)} %get-tuple-element.63), channel_id=1, source_target_pairs={{0,32},{32,64},{64,96},{96,128},{128,160},{160,192},{192,224},{224... | collective-permute-start | bytes 24584 | tf_op jit(solution)/shard_map/ppermute | solution.py:22
  218.0 13.1 %collective-permute-start.23 = (f32[4,16,16,2]{3,2,1,0:T(8,128)S(1)}, f32[4,16,16,2]{3,2,1,0:T(8,128)S(1)}, u32[]{:S(2)}, u32[]{:S(2)}) collective-permute-start(f32[4,16,16,2]{3,2,1,0:T(8,128)S(1)} %get-tuple-element.64), channel_id=1, source_target_pairs={{32,0},{64,32},{96,64},{128,96},{160,128},{192,160},{224,192},{0,2... | collective-permute-start | bytes 24584 | tf_op jit(solution)/shard_map/ppermute | solution.py:24
  243.7 14.0 %collective-permute-start.26 = (f32[4,16,16,2]{3,2,1,0:T(8,128)S(1)}, f32[4,16,16,2]{3,2,1,0:T(8,128)S(1)}, u32[]{:S(2)}, u32[]{:S(2)}) collective-permute-start(f32[4,16,16,2]{3,2,1,0:T(8,128)S(1)} %get-tuple-element.61), channel_id=1, source_target_pairs={{0,32},{32,64},{64,96},{96,128},{128,160},{160,192},{192,224},{224... | collective-permute-start | bytes 24584 | tf_op jit(solution)/shard_map/ppermute | solution.py:22
  243.8 13.9 %collective-permute-start.27 = (f32[4,16,16,2]{3,2,1,0:T(8,128)S(1)}, f32[4,16,16,2]{3,2,1,0:T(8,128)S(1)}, u32[]{:S(2)}, u32[]{:S(2)}) collective-permute-start(f32[4,16,16,2]{3,2,1,0:T(8,128)S(1)} %get-tuple-element.62), channel_id=1, source_target_pairs={{32,0},{64,32},{96,64},{128,96},{160,128},{192,160},{224,192},{0,2... | collective-permute-start | bytes 24584 | tf_op jit(solution)/shard_map/ppermute | solution.py:24
  271.7 15.2 %collective-permute-start.30 = (f32[4,16,16,2]{3,2,1,0:T(8,128)S(1)}, f32[4,16,16,2]{3,2,1,0:T(8,128)S(1)}, u32[]{:S(2)}, u32[]{:S(2)}) collective-permute-start(f32[4,16,16,2]{3,2,1,0:T(8,128)S(1)} %get-tuple-element.59), channel_id=1, source_target_pairs={{0,32},{32,64},{64,96},{96,128},{128,160},{160,192},{192,224},{224... | collective-permute-start | bytes 24584 | tf_op jit(solution)/shard_map/ppermute | solution.py:22
  271.8 15.1 %collective-permute-start.31 = (f32[4,16,16,2]{3,2,1,0:T(8,128)S(1)}, f32[4,16,16,2]{3,2,1,0:T(8,128)S(1)}, u32[]{:S(2)}, u32[]{:S(2)}) collective-permute-start(f32[4,16,16,2]{3,2,1,0:T(8,128)S(1)} %get-tuple-element.60), channel_id=1, source_target_pairs={{32,0},{64,32},{96,64},{128,96},{160,128},{192,160},{224,192},{0,2... | collective-permute-start | bytes 24584 | tf_op jit(solution)/shard_map/ppermute | solution.py:24
  287.4 15.6 %collective-permute-start.33 = (f32[4,16,2,132]{3,2,1,0:T(2,128)S(1)}, f32[4,16,2,132]{3,2,1,0:T(2,128)S(1)}, u32[]{:S(2)}, u32[]{:S(2)}) collective-permute-start(f32[4,16,2,132]{3,2,1,0:T(2,128)S(1)} %get-tuple-element.20), channel_id=1, source_target_pairs={{1,0},{2,1},{3,2},{4,3},{5,4},{6,5},{7,6},{8,7},{9,8},{10,9},{11,1... | collective-permute-start | bytes 202760 | tf_op jit(solution)/shard_map/ppermute | solution.py:24
  305.9 11.0 %collective-permute-start.34 = (f32[4,16,16,2]{3,2,1,0:T(8,128)S(1)}, f32[4,16,16,2]{3,2,1,0:T(8,128)S(1)}, u32[]{:S(2)}, u32[]{:S(2)}) collective-permute-start(f32[4,16,16,2]{3,2,1,0:T(8,128)S(1)} %get-tuple-element.57), channel_id=1, source_target_pairs={{0,32},{32,64},{64,96},{96,128},{128,160},{160,192},{192,224},{224... | collective-permute-start | bytes 24584 | tf_op jit(solution)/shard_map/ppermute | solution.py:22
  305.9 10.9 %collective-permute-start.35 = (f32[4,16,16,2]{3,2,1,0:T(8,128)S(1)}, f32[4,16,16,2]{3,2,1,0:T(8,128)S(1)}, u32[]{:S(2)}, u32[]{:S(2)}) collective-permute-start(f32[4,16,16,2]{3,2,1,0:T(8,128)S(1)} %get-tuple-element.58), channel_id=1, source_target_pairs={{32,0},{64,32},{96,64},{128,96},{160,128},{192,160},{224,192},{0,2... | collective-permute-start | bytes 24584 | tf_op jit(solution)/shard_map/ppermute | solution.py:24
  329.9 19.1 %collective-permute-start.38 = (f32[4,16,16,128]{3,2,1,0:T(8,128)S(1)}, f32[4,16,16,128]{3,2,1,0:T(8,128)S(1)}, u32[]{:S(2)}, u32[]{:S(2)}) collective-permute-start(f32[4,16,16,128]{3,2,1,0:T(8,128)S(1)} %fusion.5), channel_id=1, source_target_pairs={{0,1},{1,2},{2,3},{3,4},{4,5},{5,6},{6,7},{7,8},{8,9},{9,10},{10,1... | collective-permute-start | bytes 1572872 | tf_op jit(solution)/shard_map/ppermute | solution.py:33
  350.3 18.2 %collective-permute-start.39 = (f32[4,16,16,128]{3,2,1,0:T(8,128)S(1)}, f32[4,16,16,128]{3,2,1,0:T(8,128)S(1)}, u32[]{:S(2)}, u32[]{:S(2)}) collective-permute-start(f32[4,16,16,128]{3,2,1,0:T(8,128)S(1)} %slice_select_fusion), channel_id=1, source_target_pairs={{0,1},{1,2},{2,3},{3,4},{4,5},{5,6},{6,7},{7,8},{8,9},{9,10},{10,1... | collective-permute-start | bytes 1572872 | tf_op jit(solution)/shard_map/ppermute | solution.py:33
  368.6 16.5 %collective-permute-start.40 = (f32[4,16,16,128]{3,2,1,0:T(8,128)S(1)}, f32[4,16,16,128]{3,2,1,0:T(8,128)S(1)}, u32[]{:S(2)}, u32[]{:S(2)}) collective-permute-start(f32[4,16,16,128]{3,2,1,0:T(8,128)S(1)} %broadcast_select_fusion), channel_id=1, source_target_pairs={{0,2},{1,3},{2,4},{3,5},{4,6},{5,7},{6,8},{7,9},{8,10},{9,11},{10,... | collective-permute-start | bytes 1572872 | tf_op jit(solution)/shard_map/ppermute | solution.py:33
  385.1 15.9 %collective-permute-start.41 = (f32[4,16,16,128]{3,2,1,0:T(8,128)S(1)}, f32[4,16,16,128]{3,2,1,0:T(8,128)S(1)}, u32[]{:S(2)}, u32[]{:S(2)}) collective-permute-start(f32[4,16,16,128]{3,2,1,0:T(8,128)S(1)} %broadcast_select_fusion.2), channel_id=1, source_target_pairs={{0,4},{1,5},{2,6},{3,7},{4,8},{5,9},{6,10},{7,11},{8,12},{9,13},{1... | collective-permute-start | bytes 1572872 | tf_op jit(solution)/shard_map/ppermute | solution.py:33
  401.1 12.7 %collective-permute-start.42 = (f32[4,16,16,128]{3,2,1,0:T(8,128)S(1)}, f32[4,16,16,128]{3,2,1,0:T(8,128)S(1)}, u32[]{:S(2)}, u32[]{:S(2)}) collective-permute-start(f32[4,16,16,128]{3,2,1,0:T(8,128)S(1)} %broadcast_select_fusion.4), channel_id=1, source_target_pairs={{0,8},{1,9},{2,10},{3,11},{4,12},{5,13},{6,14},{7,15},{8,16},{9,17... | collective-permute-start | bytes 1572872 | tf_op jit(solution)/shard_map/ppermute | solution.py:33
  413.9 12.1 %collective-permute-start.43 = (f32[4,16,16,128]{3,2,1,0:T(8,128)S(1)}, f32[4,16,16,128]{3,2,1,0:T(8,128)S(1)}, u32[]{:S(2)}, u32[]{:S(2)}) collective-permute-start(f32[4,16,16,128]{3,2,1,0:T(8,128)S(1)} %broadcast_select_fusion.6), channel_id=1, source_target_pairs={{0,16},{1,17},{2,18},{3,19},{4,20},{5,21},{6,22},{7,23},{8,24},{9,... | collective-permute-start | bytes 1572872 | tf_op jit(solution)/shard_map/ppermute | solution.py:33
  (15 other events, 117.6 us)
where the time goes:
time: 436 us; the launch traced here: 427 us
  waiting for transfers between devices  305 us (70%)
  starting transfers between devices  87.3 us (20%)
  other arithmetic  22.8 us (5%)
  local copies, waits for them, and re-layouts  10.4 us (2%)
    ppermute x12, waiting for transfers between devices, shifted(): lax.ppermute(shard, axis, [(i, (i + by) % peers) for i in range(peers)])  188 us
    ppermute x16, waiting for transfers between devices, padded_2(): lax.ppermute(tail, axis, [(i, (i + 1) % count) for i in range(count)])  108 us
    ppermute x16, starting transfers between devices, padded_2(): lax.ppermute(head, axis, [((i + 1) % count, i) for i in range(count)])  66.6 us
    ppermute x16, starting transfers between devices, padded_2(): lax.ppermute(tail, axis, [(i, (i + 1) % count) for i in range(count)])  19.6 us
    ppermute x16, waiting for transfers between devices, padded_2(): lax.ppermute(head, axis, [((i + 1) % count, i) for i in range(count)])  9.46 us
  transfers between devices with their start and end apart: 44, of which 30 were waited for; matrix products, arithmetic and copies ran while one was open for 0% of the time, Pallas kernels for 0%

commit v1 on v0

v1 whole, which is shorter than its diff:
```python
import jax
import jax.numpy as jnp
from jax import lax
from jax.sharding import PartitionSpec as P

ORDER = 4
STEPS = 2


TIME_STEP = 0.5
ANGULAR_RATE = 1.0
SHEAR_RATE = 1.5


def ring(axis, by):
    count = lax.axis_size(axis)
    return [(i, (i + by) % count) for i in range(count)]


def window(values, start, length, which_dim):
    return lax.slice_in_dim(values, start, start + length, axis=which_dim)


def diff_along(values, which_dim):
    length = values.shape[which_dim] - 4
    return (
        8.0 * (window(values, 3, length, which_dim) - window(values, 1, length, which_dim))
        - (window(values, 4, length, which_dim) - window(values, 0, length, which_dim))
    ) / 12.0


def diff_vertical(values):
    return (
        8.0 * (jnp.roll(values, -1, 0) - jnp.roll(values, 1, 0))
        - (jnp.roll(values, -2, 0) - jnp.roll(values, 2, 0))
    ) / 12.0


def halos(pressure, radial_flow, azimuth_flow):
    rad_cells = jnp.stack([pressure, radial_flow])
    azi_cells = jnp.stack([pressure, azimuth_flow])
    rows = rad_cells.shape[3]
    cells = azi_cells.shape[2]
    rad_tail = lax.ppermute(rad_cells[..., rows - 2:], "rad", ring("rad", 1))
    rad_head = lax.ppermute(rad_cells[..., :2], "rad", ring("rad", -1))
    azi_tail = lax.ppermute(azi_cells[:, :, cells - 2:, :], "azi", ring("azi", 1))
    azi_head = lax.ppermute(azi_cells[:, :, :2, :], "azi", ring("azi", -1))
    rad_index = lax.axis_index("rad")
    rad_tail = jnp.where(rad_index == 0, 0.0, rad_tail)
    rad_head = jnp.where(rad_index == lax.axis_size("rad") - 1, 0.0, rad_head)
    rad_padded = jnp.concatenate([rad_tail, rad_cells, rad_head], axis=3)
    azi_padded = jnp.concatenate([azi_tail, azi_cells, azi_head], axis=2)
    return rad_padded, azi_padded


def operator(series, sound_sq):
    pressure = sound_sq * series[0]
    radial_flow, azimuth_flow, vertical_flow = series[1], series[2], series[3]
    rad_padded, azi_padded = halos(pressure, radial_flow, azimuth_flow)
    density_rate = -(
        diff_along(rad_padded[1], 2) + diff_along(azi_padded[1], 1) + diff_vertical(vertical_flow)
    )
    radial_rate = -diff_along(rad_padded[0], 2) + 2.0 * ANGULAR_RATE * azimuth_flow
    azimuth_rate = -diff_along(azi_padded[0], 1) - (2.0 - SHEAR_RATE) * ANGULAR_RATE * radial_flow
    vertical_rate = -diff_vertical(pressure)
    return jnp.stack([density_rate, radial_rate, azimuth_rate, vertical_rate])


def taylor(state, sound_sq):
    running = state
    series = state
    for degree in range(1, ORDER + 1):
        series = TIME_STEP / degree * operator(series, sound_sq)
        running = running + series
    return running


def remap(state, offsets):
    fields, depth, cells, rows = state.shape
    planes = state.reshape(fields * depth, cells, rows)
    whole = lax.all_to_all(planes, "azi", 0, 1, tiled=True)
    total = whole.shape[1]
    for bit_pos in range((total - 1).bit_length()):
        chosen = (offsets >> bit_pos) & 1 == 1
        whole = jnp.where(chosen[None, None, :], jnp.roll(whole, 1 << bit_pos, axis=1), whole)
    planes = lax.all_to_all(whole, "azi", 1, 0, tiled=True)
    return planes.reshape(fields, depth, cells, rows)


def per_device(gas_state, sound_sq, offsets):
    state = gas_state
    for timestep in range(STEPS):
        running = taylor(state, sound_sq)
        state = remap(running, offsets)
    return state


def solution(mesh):
    in_specs = (P(None, None, "azi", "rad"), P(None, "azi", "rad"), P("rad"))
    out_specs = P(None, None, "azi", "rad")
    return jax.shard_map(
        per_device, mesh=mesh, in_specs=in_specs, out_specs=out_specs, check_vma=False
    )
```

time: 436 us -> 201 us (0.46)
  the two profiles are of different devices: /device:TPU:64 before, /device:TPU:1 now
where the time goes in v1:
time: 201 us; the launch traced here: 198 us
  starting transfers between devices  69.6 us (35%)
  waiting for transfers between devices  62.4 us (31%)
  blocking collectives  46.8 us (23%)
  other arithmetic  11.2 us (6%)
  local copies, waits for them, and re-layouts  5.75 us (3%)
    ppermute x8, starting transfers between devices, halos(): rad_head = lax.ppermute(rad_cells[..., :2], 'rad', ring('rad', -1))  36.1 us
    all_to_all x2, blocking collectives, remap(): planes = lax.all_to_all(whole, 'azi', 1, 0, tiled=True)  30.1 us
    ppermute x8, waiting for transfers between devices, halos(): lax.ppermute(azi_cells[:, :, cells - 2:, :], 'azi', ring('azi', 1))  21 us
    ppermute x8, starting transfers between devices, halos(): azi_head = lax.ppermute(azi_cells[:, :, :2, :], 'azi', ring('azi', -1))  20.7 us
    ppermute x8, waiting for transfers between devices, halos(): rad_head = lax.ppermute(rad_cells[..., :2], 'rad', ring('rad', -1))  19.5 us
    all_to_all x1, blocking collectives, remap(): whole = lax.all_to_all(planes, 'azi', 0, 1, tiled=True)  16.8 us
    all_to_all x1, waiting for transfers between devices, remap(): whole = lax.all_to_all(planes, 'azi', 0, 1, tiled=True)  12.7 us
    ppermute x8, waiting for transfers between devices, halos(): rad_tail = lax.ppermute(rad_cells[..., rows - 2:], 'rad', ring('rad', 1))  8.66 us
  transfers between devices with their start and end apart: 33, of which 22 were waited for; matrix products, arithmetic and copies ran while one was open for 2% of the time, Pallas kernels for 0%

profile of v1, /device:TPU:1, one launch (start us, length us, event | category | flops | bytes accessed | tf_op | source)
XLA Modules:
  0.0 197.7 jit_solution(15282048288307847040)
XLA Ops:
  2.1 3.3 %collective-permute-start.1 = (f32[2,16,16,2]{3,2,1,0:T(8,128)S(1)}, f32[2,16,16,2]{3,2,1,0:T(8,128)S(1)}, u32[]{:S(2)}, u32[]{:S(2)}) collective-permute-start(f32[2,16,16,2]{3,2,1,0:T(8,128)S(1)} %get-tuple-element.164), channel_id=1, source_target_pairs={{0,224},{32,0},{64,32},{96,64},{128,96},{160,128},{192,160},{224,1... | collective-permute-start | bytes 12296 | tf_op jit(solution)/shard_map/ppermute | solution.py:45
  6.7 6.4 %collective-permute-start.3 = (f32[2,16,2,128]{3,2,1,0:T(2,128)S(1)}, f32[2,16,2,128]{3,2,1,0:T(2,128)S(1)}, u32[]{:S(2)}, u32[]{:S(2)}) collective-permute-start(f32[2,16,2,128]{3,2,1,0:T(2,128)S(1)} %get-tuple-element.166), channel_id=1, source_target_pairs={{0,31},{1,0},{2,1},{3,2},{4,3},{5,4},{6,5},{7,6},{8,7},{9,8},{10,9... | collective-permute-start | bytes 98312 | tf_op jit(solution)/shard_map/ppermute | solution.py:47
  14.6 5.8 %collective-permute-done.2 = f32[2,16,2,128]{3,2,1,0:T(2,128)S(1)} collective-permute-done((f32[2,16,2,128]{3,2,1,0:T(2,128)S(1)}, f32[2,16,2,128]{3,2,1,0:T(2,128)S(1)}, u32[]{:S(2)}, u32[]{:S(2)}) %collective-permute-start.2) | collective-permute-done | bytes 32800 | tf_op jit(solution)/shard_map/ppermute | solution.py:46
  21.2 3.0 %collective-permute-start.5 = (f32[2,16,16,2]{3,2,1,0:T(8,128)S(1)}, f32[2,16,16,2]{3,2,1,0:T(8,128)S(1)}, u32[]{:S(2)}, u32[]{:S(2)}) collective-permute-start(f32[2,16,16,2]{3,2,1,0:T(8,128)S(1)} %get-tuple-element.160), channel_id=1, source_target_pairs={{0,224},{32,0},{64,32},{96,64},{128,96},{160,128},{192,160},{224,1... | collective-permute-start | bytes 12296 | tf_op jit(solution)/shard_map/ppermute | solution.py:45
  25.9 2.4 %collective-permute-done.5 = f32[2,16,16,2]{3,2,1,0:T(8,128)S(1)} collective-permute-done((f32[2,16,16,2]{3,2,1,0:T(8,128)S(1)}, f32[2,16,16,2]{3,2,1,0:T(8,128)S(1)}, u32[]{:S(2)}, u32[]{:S(2)}) %collective-permute-start.5) | collective-permute-done | bytes 4128 | tf_op jit(solution)/shard_map/ppermute | solution.py:45
  28.3 2.8 %collective-permute-done.4 = f32[2,16,16,2]{3,2,1,0:T(8,128)S(1)} collective-permute-done((f32[2,16,16,2]{3,2,1,0:T(8,128)S(1)}, f32[2,16,16,2]{3,2,1,0:T(8,128)S(1)}, u32[]{:S(2)}, u32[]{:S(2)}) %collective-permute-start.4) | collective-permute-done | bytes 4128 | tf_op jit(solution)/shard_map/ppermute | solution.py:44
  33.6 3.4 %collective-permute-start.9 = (f32[2,16,16,2]{3,2,1,0:T(8,128)S(1)}, f32[2,16,16,2]{3,2,1,0:T(8,128)S(1)}, u32[]{:S(2)}, u32[]{:S(2)}) collective-permute-start(f32[2,16,16,2]{3,2,1,0:T(8,128)S(1)} %get-tuple-element.156), channel_id=1, source_target_pairs={{0,224},{32,0},{64,32},{96,64},{128,96},{160,128},{192,160},{224,1... | collective-permute-start | bytes 12296 | tf_op jit(solution)/shard_map/ppermute | solution.py:45
  37.0 4.2 %collective-permute-start.11 = (f32[2,16,2,128]{3,2,1,0:T(2,128)S(1)}, f32[2,16,2,128]{3,2,1,0:T(2,128)S(1)}, u32[]{:S(2)}, u32[]{:S(2)}) collective-permute-start(f32[2,16,2,128]{3,2,1,0:T(2,128)S(1)} %get-tuple-element.158), channel_id=1, source_target_pairs={{0,31},{1,0},{2,1},{3,2},{4,3},{5,4},{6,5},{7,6},{8,7},{9,8},{10,9... | collective-permute-start | bytes 98312 | tf_op jit(solution)/shard_map/ppermute | solution.py:47
  44.2 4.3 %collective-permute-done.10 = f32[2,16,2,128]{3,2,1,0:T(2,128)S(1)} collective-permute-done((f32[2,16,2,128]{3,2,1,0:T(2,128)S(1)}, f32[2,16,2,128]{3,2,1,0:T(2,128)S(1)}, u32[]{:S(2)}, u32[]{:S(2)}) %collective-permute-start.10) | collective-permute-done | bytes 32800 | tf_op jit(solution)/shard_map/ppermute | solution.py:46
  52.1 1.9 collective-permute-start.15
  54.1 2.7 %collective-permute-done.13 = f32[2,16,16,2]{3,2,1,0:T(8,128)S(1)} collective-permute-done((f32[2,16,16,2]{3,2,1,0:T(8,128)S(1)}, f32[2,16,16,2]{3,2,1,0:T(8,128)S(1)}, u32[]{:S(2)}, u32[]{:S(2)}) %collective-permute-start.13) | collective-permute-done | bytes 4128 | tf_op jit(solution)/shard_map/ppermute | solution.py:45
  56.8 2.1 %collective-permute-done.12 = f32[2,16,16,2]{3,2,1,0:T(8,128)S(1)} collective-permute-done((f32[2,16,16,2]{3,2,1,0:T(8,128)S(1)}, f32[2,16,16,2]{3,2,1,0:T(8,128)S(1)}, u32[]{:S(2)}, u32[]{:S(2)}) %collective-permute-start.12) | collective-permute-done | bytes 4128 | tf_op jit(solution)/shard_map/ppermute | solution.py:44
  59.3 1.8 collective-permute-done.14
  62.5 6.2 %all-to-all-start = ((f32[64,16,128]{2,1,0:T(8,128)}), f32[64,16,128]{2,1,0:T(8,128)S(1)}, u32[]{:S(2)}, u32[]{:S(2)}) async-start(f32[64,16,128]{2,1,0:T(8,128)} %bitcast.108), calls=%async_computation | async-start | bytes 1048576 | tf_op jit(solution)/shard_map/all_to_all | solution.py:81
  68.7 12.7 %all-to-all-done = f32[64,16,128]{2,1,0:T(8,128)S(1)} async-done(((f32[64,16,128]{2,1,0:T(8,128)}), f32[64,16,128]{2,1,0:T(8,128)S(1)}, u32[]{:S(2)}, u32[]{:S(2)}) %all-to-all-start) | async-done | bytes 524320 | tf_op jit(solution)/shard_map/all_to_all | solution.py:81
  82.8 14.7 %all_to_all.66 = f32[2,512,128]{2,0,1:T(2,128)S(1)} all-to-all(f32[2,512,128]{2,0,1:T(2,128)S(1)} %copy.17), channel_id=1, replica_groups=mesh['rad'=8,'azi'=32] {'azi'}, dimensions={1} | all-to-all | bytes 1048576 | tf_op jit(solution)/shard_map/all_to_all | solution.py:86
  97.9 1.9 collective-permute-start.17
  103.2 4.5 %collective-permute-done.17 = f32[2,16,16,2]{3,2,1,0:T(8,128)S(1)} collective-permute-done((f32[2,16,16,2]{3,2,1,0:T(8,128)S(1)}, f32[2,16,16,2]{3,2,1,0:T(8,128)S(1)}, u32[]{:S(2)}, u32[]{:S(2)}) %collective-permute-start.17) | collective-permute-done | bytes 4128 | tf_op jit(solution)/shard_map/ppermute | solution.py:45
  109.8 14.5 %collective-permute-start.21 = (f32[2,16,16,2]{3,2,1,0:T(8,128)S(1)}, f32[2,16,16,2]{3,2,1,0:T(8,128)S(1)}, u32[]{:S(2)}, u32[]{:S(2)}) collective-permute-start(f32[2,16,16,2]{3,2,1,0:T(8,128)S(1)} %get-tuple-element.144), channel_id=1, source_target_pairs={{0,224},{32,0},{64,32},{96,64},{128,96},{160,128},{192,160},{224,1... | collective-permute-start | bytes 12296 | tf_op jit(solution)/shard_map/ppermute | solution.py:45
  124.2 3.2 %collective-permute-start.23 = (f32[2,16,2,128]{3,2,1,0:T(2,128)S(1)}, f32[2,16,2,128]{3,2,1,0:T(2,128)S(1)}, u32[]{:S(2)}, u32[]{:S(2)}) collective-permute-start(f32[2,16,2,128]{3,2,1,0:T(2,128)S(1)} %get-tuple-element.146), channel_id=1, source_target_pairs={{0,31},{1,0},{2,1},{3,2},{4,3},{5,4},{6,5},{7,6},{8,7},{9,8},{10,9... | collective-permute-start | bytes 98312 | tf_op jit(solution)/shard_map/ppermute | solution.py:47
  127.5 2.2 %collective-permute-done.21 = f32[2,16,16,2]{3,2,1,0:T(8,128)S(1)} collective-permute-done((f32[2,16,16,2]{3,2,1,0:T(8,128)S(1)}, f32[2,16,16,2]{3,2,1,0:T(8,128)S(1)}, u32[]{:S(2)}, u32[]{:S(2)}) %collective-permute-start.21) | collective-permute-done | bytes 4128 | tf_op jit(solution)/shard_map/ppermute | solution.py:45
  130.1 4.3 %collective-permute-done.22 = f32[2,16,2,128]{3,2,1,0:T(2,128)S(1)} collective-permute-done((f32[2,16,2,128]{3,2,1,0:T(2,128)S(1)}, f32[2,16,2,128]{3,2,1,0:T(2,128)S(1)}, u32[]{:S(2)}, u32[]{:S(2)}) %collective-permute-start.22) | collective-permute-done | bytes 32800 | tf_op jit(solution)/shard_map/ppermute | solution.py:46
  135.3 2.0 %collective-permute-start.25 = (f32[2,16,16,2]{3,2,1,0:T(8,128)S(1)}, f32[2,16,16,2]{3,2,1,0:T(8,128)S(1)}, u32[]{:S(2)}, u32[]{:S(2)}) collective-permute-start(f32[2,16,16,2]{3,2,1,0:T(8,128)S(1)} %get-tuple-element.140), channel_id=1, source_target_pairs={{0,224},{32,0},{64,32},{96,64},{128,96},{160,128},{192,160},{224,1... | collective-permute-start | bytes 12296 | tf_op jit(solution)/shard_map/ppermute | solution.py:45
  139.6 3.5 %collective-permute-done.25 = f32[2,16,16,2]{3,2,1,0:T(8,128)S(1)} collective-permute-done((f32[2,16,16,2]{3,2,1,0:T(8,128)S(1)}, f32[2,16,16,2]{3,2,1,0:T(8,128)S(1)}, u32[]{:S(2)}, u32[]{:S(2)}) %collective-permute-start.25) | collective-permute-done | bytes 4128 | tf_op jit(solution)/shard_map/ppermute | solution.py:45
  143.1 1.8 collective-permute-done.24
  146.4 6.4 %collective-permute-start.29 = (f32[2,16,16,2]{3,2,1,0:T(8,128)S(1)}, f32[2,16,16,2]{3,2,1,0:T(8,128)S(1)}, u32[]{:S(2)}, u32[]{:S(2)}) collective-permute-start(f32[2,16,16,2]{3,2,1,0:T(8,128)S(1)} %get-tuple-element.136), channel_id=1, source_target_pairs={{0,224},{32,0},{64,32},{96,64},{128,96},{160,128},{192,160},{224,1... | collective-permute-start | bytes 12296 | tf_op jit(solution)/shard_map/ppermute | solution.py:45
  152.8 2.2 %collective-permute-start.31 = (f32[2,16,2,128]{3,2,1,0:T(2,128)S(1)}, f32[2,16,2,128]{3,2,1,0:T(2,128)S(1)}, u32[]{:S(2)}, u32[]{:S(2)}) collective-permute-start(f32[2,16,2,128]{3,2,1,0:T(2,128)S(1)} %get-tuple-element.138), channel_id=1, source_target_pairs={{0,31},{1,0},{2,1},{3,2},{4,3},{5,4},{6,5},{7,6},{8,7},{9,8},{10,9... | collective-permute-start | bytes 98312 | tf_op jit(solution)/shard_map/ppermute | solution.py:47
  155.1 2.6 %collective-permute-done.29 = f32[2,16,16,2]{3,2,1,0:T(8,128)S(1)} collective-permute-done((f32[2,16,16,2]{3,2,1,0:T(8,128)S(1)}, f32[2,16,16,2]{3,2,1,0:T(8,128)S(1)}, u32[]{:S(2)}, u32[]{:S(2)}) %collective-permute-start.29) | collective-permute-done | bytes 4128 | tf_op jit(solution)/shard_map/ppermute | solution.py:45
  157.8 1.8 collective-permute-done.28
  159.9 2.5 %collective-permute-done.30 = f32[2,16,2,128]{3,2,1,0:T(2,128)S(1)} collective-permute-done((f32[2,16,2,128]{3,2,1,0:T(2,128)S(1)}, f32[2,16,2,128]{3,2,1,0:T(2,128)S(1)}, u32[]{:S(2)}, u32[]{:S(2)}) %collective-permute-start.30) | collective-permute-done | bytes 32800 | tf_op jit(solution)/shard_map/ppermute | solution.py:46
  163.1 16.8 %all_to_all.67 = f32[64,16,128]{2,1,0:T(8,128)S(1)} all-to-all(f32[64,16,128]{2,1,0:T(8,128)S(1)} %bitcast_add_fusion), channel_id=1, replica_groups=mesh['rad'=8,'azi'=32] {'azi'}, dimensions={0} | all-to-all | bytes 1048576 | tf_op jit(solution)/shard_map/all_to_all | solution.py:81
  181.3 15.4 %all_to_all.68 = f32[2,512,128]{2,0,1:T(2,128)S(1)} all-to-all(f32[2,512,128]{2,0,1:T(2,128)S(1)} %copy.29), channel_id=1, replica_groups=mesh['rad'=8,'azi'=32] {'azi'}, dimensions={1} | all-to-all | bytes 1048576 | tf_op jit(solution)/shard_map/all_to_all | solution.py:86
  (283 shorter events, 32.9 us)
Async XLA Ops:
  2.1 12.1 %collective-permute-start.1 = (f32[2,16,16,2]{3,2,1,0:T(8,128)S(1)}, f32[2,16,16,2]{3,2,1,0:T(8,128)S(1)}, u32[]{:S(2)}, u32[]{:S(2)}) collective-permute-start(f32[2,16,16,2]{3,2,1,0:T(8,128)S(1)} %get-tuple-element.164), channel_id=1, source_target_pairs={{0,224},{32,0},{64,32},{96,64},{128,96},{160,128},{192,160},{224,1... | collective-permute-start | bytes 12296 | tf_op jit(solution)/shard_map/ppermute | solution.py:45
  5.4 8.9 %collective-permute-start = (f32[2,16,16,2]{3,2,1,0:T(8,128)S(1)}, f32[2,16,16,2]{3,2,1,0:T(8,128)S(1)}, u32[]{:S(2)}, u32[]{:S(2)}) collective-permute-start(f32[2,16,16,2]{3,2,1,0:T(8,128)S(1)} %get-tuple-element.163), channel_id=1, source_target_pairs={{0,32},{32,64},{64,96},{96,128},{128,160},{160,192},{192,224},{224... | collective-permute-start | bytes 12296 | tf_op jit(solution)/shard_map/ppermute | solution.py:44
  6.7 7.9 %collective-permute-start.3 = (f32[2,16,2,128]{3,2,1,0:T(2,128)S(1)}, f32[2,16,2,128]{3,2,1,0:T(2,128)S(1)}, u32[]{:S(2)}, u32[]{:S(2)}) collective-permute-start(f32[2,16,2,128]{3,2,1,0:T(2,128)S(1)} %get-tuple-element.166), channel_id=1, source_target_pairs={{0,31},{1,0},{2,1},{3,2},{4,3},{5,4},{6,5},{7,6},{8,7},{9,8},{10,9... | collective-permute-start | bytes 98312 | tf_op jit(solution)/shard_map/ppermute | solution.py:47
  13.0 7.3 %collective-permute-start.2 = (f32[2,16,2,128]{3,2,1,0:T(2,128)S(1)}, f32[2,16,2,128]{3,2,1,0:T(2,128)S(1)}, u32[]{:S(2)}, u32[]{:S(2)}) collective-permute-start(f32[2,16,2,128]{3,2,1,0:T(2,128)S(1)} %get-tuple-element.165), channel_id=1, source_target_pairs={{0,1},{1,2},{2,3},{3,4},{4,5},{5,6},{6,7},{7,8},{8,9},{9,10},{10,1... | collective-permute-start | bytes 98312 | tf_op jit(solution)/shard_map/ppermute | solution.py:46
  21.2 7.0 %collective-permute-start.5 = (f32[2,16,16,2]{3,2,1,0:T(8,128)S(1)}, f32[2,16,16,2]{3,2,1,0:T(8,128)S(1)}, u32[]{:S(2)}, u32[]{:S(2)}) collective-permute-start(f32[2,16,16,2]{3,2,1,0:T(8,128)S(1)} %get-tuple-element.160), channel_id=1, source_target_pairs={{0,224},{32,0},{64,32},{96,64},{128,96},{160,128},{192,160},{224,1... | collective-permute-start | bytes 12296 | tf_op jit(solution)/shard_map/ppermute | solution.py:45
  24.3 6.8 %collective-permute-start.4 = (f32[2,16,16,2]{3,2,1,0:T(8,128)S(1)}, f32[2,16,16,2]{3,2,1,0:T(8,128)S(1)}, u32[]{:S(2)}, u32[]{:S(2)}) collective-permute-start(f32[2,16,16,2]{3,2,1,0:T(8,128)S(1)} %get-tuple-element.159), channel_id=1, source_target_pairs={{0,32},{32,64},{64,96},{96,128},{128,160},{160,192},{192,224},{224... | collective-permute-start | bytes 12296 | tf_op jit(solution)/shard_map/ppermute | solution.py:44
  24.3 7.1 %collective-permute-start.7 = (f32[2,16,2,128]{3,2,1,0:T(2,128)S(1)}, f32[2,16,2,128]{3,2,1,0:T(2,128)S(1)}, u32[]{:S(2)}, u32[]{:S(2)}) collective-permute-start(f32[2,16,2,128]{3,2,1,0:T(2,128)S(1)} %get-tuple-element.162), channel_id=1, source_target_pairs={{0,31},{1,0},{2,1},{3,2},{4,3},{5,4},{6,5},{7,6},{8,7},{9,8},{10,9... | collective-permute-start | bytes 98312 | tf_op jit(solution)/shard_map/ppermute | solution.py:47
  25.4 7.3 %collective-permute-start.6 = (f32[2,16,2,128]{3,2,1,0:T(2,128)S(1)}, f32[2,16,2,128]{3,2,1,0:T(2,128)S(1)}, u32[]{:S(2)}, u32[]{:S(2)}) collective-permute-start(f32[2,16,2,128]{3,2,1,0:T(2,128)S(1)} %get-tuple-element.161), channel_id=1, source_target_pairs={{0,1},{1,2},{2,3},{3,4},{4,5},{5,6},{6,7},{7,8},{8,9},{9,10},{10,1... | collective-permute-start | bytes 98312 | tf_op jit(solution)/shard_map/ppermute | solution.py:46
  33.6 9.7 %collective-permute-start.9 = (f32[2,16,16,2]{3,2,1,0:T(8,128)S(1)}, f32[2,16,16,2]{3,2,1,0:T(8,128)S(1)}, u32[]{:S(2)}, u32[]{:S(2)}) collective-permute-start(f32[2,16,16,2]{3,2,1,0:T(8,128)S(1)} %get-tuple-element.156), channel_id=1, source_target_pairs={{0,224},{32,0},{64,32},{96,64},{128,96},{160,128},{192,160},{224,1... | collective-permute-start | bytes 12296 | tf_op jit(solution)/shard_map/ppermute | solution.py:45
  37.0 6.4 %collective-permute-start.8 = (f32[2,16,16,2]{3,2,1,0:T(8,128)S(1)}, f32[2,16,16,2]{3,2,1,0:T(8,128)S(1)}, u32[]{:S(2)}, u32[]{:S(2)}) collective-permute-start(f32[2,16,16,2]{3,2,1,0:T(8,128)S(1)} %get-tuple-element.155), channel_id=1, source_target_pairs={{0,32},{32,64},{64,96},{96,128},{128,160},{160,192},{192,224},{224... | collective-permute-start | bytes 12296 | tf_op jit(solution)/shard_map/ppermute | solution.py:44
  37.0 7.2 %collective-permute-start.11 = (f32[2,16,2,128]{3,2,1,0:T(2,128)S(1)}, f32[2,16,2,128]{3,2,1,0:T(2,128)S(1)}, u32[]{:S(2)}, u32[]{:S(2)}) collective-permute-start(f32[2,16,2,128]{3,2,1,0:T(2,128)S(1)} %get-tuple-element.158), channel_id=1, source_target_pairs={{0,31},{1,0},{2,1},{3,2},{4,3},{5,4},{6,5},{7,6},{8,7},{9,8},{10,9... | collective-permute-start | bytes 98312 | tf_op jit(solution)/shard_map/ppermute | solution.py:47
  41.3 7.2 %collective-permute-start.10 = (f32[2,16,2,128]{3,2,1,0:T(2,128)S(1)}, f32[2,16,2,128]{3,2,1,0:T(2,128)S(1)}, u32[]{:S(2)}, u32[]{:S(2)}) collective-permute-start(f32[2,16,2,128]{3,2,1,0:T(2,128)S(1)} %get-tuple-element.157), channel_id=1, source_target_pairs={{0,1},{1,2},{2,3},{3,4},{4,5},{5,6},{6,7},{7,8},{8,9},{9,10},{10,1... | collective-permute-start | bytes 98312 | tf_op jit(solution)/shard_map/ppermute | solution.py:46
  49.4 7.4 %collective-permute-start.13 = (f32[2,16,16,2]{3,2,1,0:T(8,128)S(1)}, f32[2,16,16,2]{3,2,1,0:T(8,128)S(1)}, u32[]{:S(2)}, u32[]{:S(2)}) collective-permute-start(f32[2,16,16,2]{3,2,1,0:T(8,128)S(1)} %get-tuple-element.152), channel_id=1, source_target_pairs={{0,224},{32,0},{64,32},{96,64},{128,96},{160,128},{192,160},{224,1... | collective-permute-start | bytes 12296 | tf_op jit(solution)/shard_map/ppermute | solution.py:45
  51.0 7.9 %collective-permute-start.12 = (f32[2,16,16,2]{3,2,1,0:T(8,128)S(1)}, f32[2,16,16,2]{3,2,1,0:T(8,128)S(1)}, u32[]{:S(2)}, u32[]{:S(2)}) collective-permute-start(f32[2,16,16,2]{3,2,1,0:T(8,128)S(1)} %get-tuple-element.151), channel_id=1, source_target_pairs={{0,32},{32,64},{64,96},{96,128},{128,160},{160,192},{192,224},{224... | collective-permute-start | bytes 12296 | tf_op jit(solution)/shard_map/ppermute | solution.py:44
  52.1 7.1 %collective-permute-start.15 = (f32[2,16,2,128]{3,2,1,0:T(2,128)S(1)}, f32[2,16,2,128]{3,2,1,0:T(2,128)S(1)}, u32[]{:S(2)}, u32[]{:S(2)}) collective-permute-start(f32[2,16,2,128]{3,2,1,0:T(2,128)S(1)} %get-tuple-element.154), channel_id=1, source_target_pairs={{0,31},{1,0},{2,1},{3,2},{4,3},{5,4},{6,5},{7,6},{8,7},{9,8},{10,9... | collective-permute-start | bytes 98312 | tf_op jit(solution)/shard_map/ppermute | solution.py:47
  54.0 7.0 %collective-permute-start.14 = (f32[2,16,2,128]{3,2,1,0:T(2,128)S(1)}, f32[2,16,2,128]{3,2,1,0:T(2,128)S(1)}, u32[]{:S(2)}, u32[]{:S(2)}) collective-permute-start(f32[2,16,2,128]{3,2,1,0:T(2,128)S(1)} %get-tuple-element.153), channel_id=1, source_target_pairs={{0,1},{1,2},{2,3},{3,4},{4,5},{5,6},{6,7},{7,8},{8,9},{9,10},{10,1... | collective-permute-start | bytes 98312 | tf_op jit(solution)/shard_map/ppermute | solution.py:46
  62.5 18.9 %all-to-all-start = ((f32[64,16,128]{2,1,0:T(8,128)}), f32[64,16,128]{2,1,0:T(8,128)S(1)}, u32[]{:S(2)}, u32[]{:S(2)}) async-start(f32[64,16,128]{2,1,0:T(8,128)} %bitcast.108), calls=%async_computation | async-start | bytes 1048576 | tf_op jit(solution)/shard_map/all_to_all | solution.py:81
  97.9 9.7 %collective-permute-start.17 = (f32[2,16,16,2]{3,2,1,0:T(8,128)S(1)}, f32[2,16,16,2]{3,2,1,0:T(8,128)S(1)}, u32[]{:S(2)}, u32[]{:S(2)}) collective-permute-start(f32[2,16,16,2]{3,2,1,0:T(8,128)S(1)} %get-tuple-element.148), channel_id=1, source_target_pairs={{0,224},{32,0},{64,32},{96,64},{128,96},{160,128},{192,160},{224,1... | collective-permute-start | bytes 12296 | tf_op jit(solution)/shard_map/ppermute | solution.py:45
  100.0 8.0 %collective-permute-start.19 = (f32[2,16,2,128]{3,2,1,0:T(2,128)S(1)}, f32[2,16,2,128]{3,2,1,0:T(2,128)S(1)}, u32[]{:S(2)}, u32[]{:S(2)}) collective-permute-start(f32[2,16,2,128]{3,2,1,0:T(2,128)S(1)} %get-tuple-element.150), channel_id=1, source_target_pairs={{0,31},{1,0},{2,1},{3,2},{4,3},{5,4},{6,5},{7,6},{8,7},{9,8},{10,9... | collective-permute-start | bytes 98312 | tf_op jit(solution)/shard_map/ppermute | solution.py:47
  101.6 7.3 %collective-permute-start.18 = (f32[2,16,2,128]{3,2,1,0:T(2,128)S(1)}, f32[2,16,2,128]{3,2,1,0:T(2,128)S(1)}, u32[]{:S(2)}, u32[]{:S(2)}) collective-permute-start(f32[2,16,2,128]{3,2,1,0:T(2,128)S(1)} %get-tuple-element.149), channel_id=1, source_target_pairs={{0,1},{1,2},{2,3},{3,4},{4,5},{5,6},{6,7},{7,8},{8,9},{9,10},{10,1... | collective-permute-start | bytes 98312 | tf_op jit(solution)/shard_map/ppermute | solution.py:46
  101.6 6.1 %collective-permute-start.16 = (f32[2,16,16,2]{3,2,1,0:T(8,128)S(1)}, f32[2,16,16,2]{3,2,1,0:T(8,128)S(1)}, u32[]{:S(2)}, u32[]{:S(2)}) collective-permute-start(f32[2,16,16,2]{3,2,1,0:T(8,128)S(1)} %get-tuple-element.147), channel_id=1, source_target_pairs={{0,32},{32,64},{64,96},{96,128},{128,160},{160,192},{192,224},{224... | collective-permute-start | bytes 12296 | tf_op jit(solution)/shard_map/ppermute | solution.py:44
  109.8 19.9 %collective-permute-start.21 = (f32[2,16,16,2]{3,2,1,0:T(8,128)S(1)}, f32[2,16,16,2]{3,2,1,0:T(8,128)S(1)}, u32[]{:S(2)}, u32[]{:S(2)}) collective-permute-start(f32[2,16,16,2]{3,2,1,0:T(8,128)S(1)} %get-tuple-element.144), channel_id=1, source_target_pairs={{0,224},{32,0},{64,32},{96,64},{128,96},{160,128},{192,160},{224,1... | collective-permute-start | bytes 12296 | tf_op jit(solution)/shard_map/ppermute | solution.py:45
  124.2 5.8 %collective-permute-start.23 = (f32[2,16,2,128]{3,2,1,0:T(2,128)S(1)}, f32[2,16,2,128]{3,2,1,0:T(2,128)S(1)}, u32[]{:S(2)}, u32[]{:S(2)}) collective-permute-start(f32[2,16,2,128]{3,2,1,0:T(2,128)S(1)} %get-tuple-element.146), channel_id=1, source_target_pairs={{0,31},{1,0},{2,1},{3,2},{4,3},{5,4},{6,5},{7,6},{8,7},{9,8},{10,9... | collective-permute-start | bytes 98312 | tf_op jit(solution)/shard_map/ppermute | solution.py:47
  127.4 7.0 %collective-permute-start.22 = (f32[2,16,2,128]{3,2,1,0:T(2,128)S(1)}, f32[2,16,2,128]{3,2,1,0:T(2,128)S(1)}, u32[]{:S(2)}, u32[]{:S(2)}) collective-permute-start(f32[2,16,2,128]{3,2,1,0:T(2,128)S(1)} %get-tuple-element.145), channel_id=1, source_target_pairs={{0,1},{1,2},{2,3},{3,4},{4,5},{5,6},{6,7},{7,8},{8,9},{9,10},{10,1... | collective-permute-start | bytes 98312 | tf_op jit(solution)/shard_map/ppermute | solution.py:46
  135.3 7.8 %collective-permute-start.25 = (f32[2,16,16,2]{3,2,1,0:T(8,128)S(1)}, f32[2,16,16,2]{3,2,1,0:T(8,128)S(1)}, u32[]{:S(2)}, u32[]{:S(2)}) collective-permute-start(f32[2,16,16,2]{3,2,1,0:T(8,128)S(1)} %get-tuple-element.140), channel_id=1, source_target_pairs={{0,224},{32,0},{64,32},{96,64},{128,96},{160,128},{192,160},{224,1... | collective-permute-start | bytes 12296 | tf_op jit(solution)/shard_map/ppermute | solution.py:45
  137.3 7.7 %collective-permute-start.24 = (f32[2,16,16,2]{3,2,1,0:T(8,128)S(1)}, f32[2,16,16,2]{3,2,1,0:T(8,128)S(1)}, u32[]{:S(2)}, u32[]{:S(2)}) collective-permute-start(f32[2,16,16,2]{3,2,1,0:T(8,128)S(1)} %get-tuple-element.139), channel_id=1, source_target_pairs={{0,32},{32,64},{64,96},{96,128},{128,160},{160,192},{192,224},{224... | collective-permute-start | bytes 12296 | tf_op jit(solution)/shard_map/ppermute | solution.py:44
  138.0 7.3 %collective-permute-start.27 = (f32[2,16,2,128]{3,2,1,0:T(2,128)S(1)}, f32[2,16,2,128]{3,2,1,0:T(2,128)S(1)}, u32[]{:S(2)}, u32[]{:S(2)}) collective-permute-start(f32[2,16,2,128]{3,2,1,0:T(2,128)S(1)} %get-tuple-element.142), channel_id=1, source_target_pairs={{0,31},{1,0},{2,1},{3,2},{4,3},{5,4},{6,5},{7,6},{8,7},{9,8},{10,9... | collective-permute-start | bytes 98312 | tf_op jit(solution)/shard_map/ppermute | solution.py:47
  138.1 7.4 %collective-permute-start.26 = (f32[2,16,2,128]{3,2,1,0:T(2,128)S(1)}, f32[2,16,2,128]{3,2,1,0:T(2,128)S(1)}, u32[]{:S(2)}, u32[]{:S(2)}) collective-permute-start(f32[2,16,2,128]{3,2,1,0:T(2,128)S(1)} %get-tuple-element.141), channel_id=1, source_target_pairs={{0,1},{1,2},{2,3},{3,4},{4,5},{5,6},{6,7},{7,8},{8,9},{9,10},{10,1... | collective-permute-start | bytes 98312 | tf_op jit(solution)/shard_map/ppermute | solution.py:46
  146.4 11.3 %collective-permute-start.29 = (f32[2,16,16,2]{3,2,1,0:T(8,128)S(1)}, f32[2,16,16,2]{3,2,1,0:T(8,128)S(1)}, u32[]{:S(2)}, u32[]{:S(2)}) collective-permute-start(f32[2,16,16,2]{3,2,1,0:T(8,128)S(1)} %get-tuple-element.136), channel_id=1, source_target_pairs={{0,224},{32,0},{64,32},{96,64},{128,96},{160,128},{192,160},{224,1... | collective-permute-start | bytes 12296 | tf_op jit(solution)/shard_map/ppermute | solution.py:45
  152.8 6.8 %collective-permute-start.28 = (f32[2,16,16,2]{3,2,1,0:T(8,128)S(1)}, f32[2,16,16,2]{3,2,1,0:T(8,128)S(1)}, u32[]{:S(2)}, u32[]{:S(2)}) collective-permute-start(f32[2,16,16,2]{3,2,1,0:T(8,128)S(1)} %get-tuple-element.135), channel_id=1, source_target_pairs={{0,32},{32,64},{64,96},{96,128},{128,160},{160,192},{192,224},{224... | collective-permute-start | bytes 12296 | tf_op jit(solution)/shard_map/ppermute | solution.py:44
  152.8 7.1 %collective-permute-start.31 = (f32[2,16,2,128]{3,2,1,0:T(2,128)S(1)}, f32[2,16,2,128]{3,2,1,0:T(2,128)S(1)}, u32[]{:S(2)}, u32[]{:S(2)}) collective-permute-start(f32[2,16,2,128]{3,2,1,0:T(2,128)S(1)} %get-tuple-element.138), channel_id=1, source_target_pairs={{0,31},{1,0},{2,1},{3,2},{4,3},{5,4},{6,5},{7,6},{8,7},{9,8},{10,9... | collective-permute-start | bytes 98312 | tf_op jit(solution)/shard_map/ppermute | solution.py:47
  155.0 7.4 %collective-permute-start.30 = (f32[2,16,2,128]{3,2,1,0:T(2,128)S(1)}, f32[2,16,2,128]{3,2,1,0:T(2,128)S(1)}, u32[]{:S(2)}, u32[]{:S(2)}) collective-permute-start(f32[2,16,2,128]{3,2,1,0:T(2,128)S(1)} %get-tuple-element.137), channel_id=1, source_target_pairs={{0,1},{1,2},{2,3},{3,4},{4,5},{5,6},{6,7},{7,8},{8,9},{9,10},{10,1... | collective-permute-start | bytes 98312 | tf_op jit(solution)/shard_map/ppermute | solution.py:46
  (4 other events, 13.7 us)
